TPU v7x, 256 devices: a whole 4x4x8 slice. The times are simulated.
256 devices in a mesh: hst: 64 (over x, z, core), local: 4 (over y).
Axes of the slice: x: 4, y: 4, z: 8, core: 2. Of those that a mesh axis runs over, the one named last changes fastest.
Arguments:
- patches: bfloat16 [262144, 768], P(('hst', 'local')), may hold values from -6 to 6
- w_in: bfloat16 [768, 3072], replicated, may hold values from -0.21875 to 0.21875
- b_in: float32 [3072], replicated, may hold values from -3 to 3
- w_out: bfloat16 [3072, 512], replicated, may hold values from -0.15625 to 0.15625
- b_out: float32 [512], replicated, may hold values from -3 to 3
- ema_sums: float32 [262144, 512], P(('hst', 'local')), may hold values from -12 to 12
- ema_counts: float32 [262144], P(('hst', 'local')), may hold values from 0.5 to 4
- code_ids: int32 [262144], P(('hst', 'local')), may hold values from 0 to 262143, as said below
Outputs:
- codebook: float32 [262144, 512], P(('hst', 'local'))
- new_counts: float32 [262144], P(('hst', 'local'))
- quantized: bfloat16 [262144, 512], P(('hst', 'local'))
Inputs may be any that keep to these rules, and one draw needn't show every extreme that they name: `code_ids`: in each aligned block of 1024 patches (the patches of one device), at most 8 ids lie in any one range [k * 1024, (k + 1) * 1024); one such range gets exactly 8 from every block.
All inputs are finite; a program needn't handle non-finite values.
Results may differ from a plain program's by a relative error of at most 0.002.
Values may be sent and summed in bfloat16 or wider, within the bound.
No kernel may reach another device: no remote copies, remote signals or barrier semaphores. Data moves between devices by JAX's collectives and lax.ppermute only.
A program may use at most 64 MiB of HBM per device.

v0:
```python
import jax
import jax.numpy as jnp
from jax import lax
from jax.sharding import PartitionSpec as P

DECAY = 0.9


def per_device(patches, w_in, b_in, w_out, b_out, ema_sums, ema_counts, code_ids):
    host_count = lax.axis_size("hst")
    local_count = lax.axis_size("local")
    owner_count = host_count * local_count
    code_span = ema_sums.shape[0]
    latent_width = ema_sums.shape[1]
    row_count = patches.shape[0]
    capacity = max(2, 2 * row_count // owner_count)
    pre_act = jnp.dot(patches, w_in, preferred_element_type=jnp.float32) + b_in
    hidden = jnp.tanh(pre_act).astype(jnp.bfloat16)
    latents = (jnp.dot(hidden, w_out, preferred_element_type=jnp.float32) + b_out).astype(
        jnp.bfloat16
    )
    owner_of = code_ids // code_span
    members = (owner_of[:, None] == jnp.arange(owner_count)[None, :]).astype(jnp.int32)
    running = jnp.cumsum(members, axis=0)
    position = jnp.sum(running * members, axis=1) - 1
    slot_index = owner_of * capacity + position
    placing = jnp.arange(owner_count * capacity)[:, None] == slot_index[None, :]
    outgoing = jnp.dot(
        placing.astype(jnp.bfloat16), latents, preferred_element_type=jnp.float32
    ).astype(jnp.bfloat16)
    sent_ids = jnp.max(jnp.where(placing, code_ids[None, :], -1), axis=1)
    outgoing = outgoing.reshape(host_count, local_count, capacity, latent_width)
    sent_ids = sent_ids.reshape(host_count, local_count, capacity)
    halfway = (
        lax.all_to_all(outgoing, "hst", split_axis=0, concat_axis=0, tiled=True),
        lax.all_to_all(sent_ids, "hst", split_axis=0, concat_axis=0, tiled=True),
    )
    arrived, arrived_ids = (
        lax.all_to_all(halfway[0], "local", split_axis=1, concat_axis=1, tiled=True),
        lax.all_to_all(halfway[1], "local", split_axis=1, concat_axis=1, tiled=True),
    )
    arrived = arrived.reshape(owner_count * capacity, latent_width)
    arrived_ids = arrived_ids.reshape(owner_count * capacity)
    first_code = (lax.axis_index("hst") * local_count + lax.axis_index("local")) * code_span
    offset_code = arrived_ids - first_code
    chosen = (offset_code[:, None] == jnp.arange(code_span)[None, :]).astype(jnp.bfloat16)
    code_sums = lax.dot_general(
        chosen, arrived, (((0,), (0,)), ((), ())), preferred_element_type=jnp.float32
    )
    code_counts = jnp.sum(chosen, axis=0, dtype=jnp.float32)
    new_counts = DECAY * ema_counts + (1.0 - DECAY) * code_counts
    codebook = (DECAY * ema_sums + (1.0 - DECAY) * code_sums) / new_counts[:, None]
    replies = jnp.dot(
        chosen, codebook.astype(jnp.bfloat16), preferred_element_type=jnp.float32
    ).astype(jnp.bfloat16)
    replies = replies.reshape(host_count, local_count, capacity, latent_width)
    returned = lax.all_to_all(
        lax.all_to_all(replies, "hst", split_axis=0, concat_axis=0, tiled=True),
        "local",
        split_axis=1,
        concat_axis=1,
        tiled=True,
    )
    back_rows = returned.reshape(owner_count * capacity, latent_width)
    quantized = jnp.take(back_rows, slot_index, axis=0)
    return (codebook, new_counts, quantized)


def solution(mesh):
    in_specs = (
        P(("hst", "local"), None),
        P(),
        P(),
        P(),
        P(),
        P(("hst", "local"), None),
        P(("hst", "local")),
        P(("hst", "local")),
    )
    out_specs = (P(("hst", "local"), None), P(("hst", "local")), P(("hst", "local"), None))
    return jax.shard_map(
        per_device, mesh=mesh, in_specs=in_specs, out_specs=out_specs, check_vma=False
    )
```

profile of v0, /device:TPU:1, one launch (start us, length us, event | category | flops | bytes accessed | tf_op | source)
XLA Modules:
  0.0 247.7 jit_solution(14626042498962220828)
XLA Ops:
  0.6 0.8 add_select_fusion
  1.6 0.2 fusion.15
  1.8 1.0 copy-done.1
  2.8 1.3 broadcast_add_fusion
  4.2 0.3 copy.37
  4.5 0.4 fusion.13
  4.9 1.2 select_reduce_fusion
  6.1 0.8 reshape.56
  6.9 13.0 %all-to-all-start = ((s32[64,4,8]{2,1,0:T(4,128)}), s32[64,4,8]{2,1,0:T(4,128)S(1)}, u32[]{:S(2)}, u32[]{:S(2)}) async-start(s32[64,4,8]{2,1,0:T(4,128)} %reshape.56), calls=%async_computation | async-start | bytes 262144 | tf_op jit(solution)/shard_map/all_to_all | solution.py:36
  19.9 12.1 %add_convert_fusion = bf16[1024,512]{1,0:T(8,128)(2,1)} fusion(bf16[3072,512]{1,0:T(8,128)(2,1)S(1)} %copy-done, f32[3072]{0:T(1024)S(1)} %copy-done.6, bf16[1024,768]{1,0:T(8,128)(2,1)} %param.8, bf16[768,3072]{1,0:T(8,128)(2,1)} %param.9, f32[512]{0:T(512)S(1)} %copy-done.7), kind=kOutput, calls=%fused_computation.19 | convolution fusion | flops 8060403712 | bytes 10500096 | tf_op jit(solution)/shard_map/dot_general | solution.py:19
  32.0 4.9 %fusion.10 = bf16[2048,512]{1,0:T(8,128)(2,1)} fusion(bf16[1024,512]{1,0:T(8,128)(2,1)} %add_convert_fusion, s32[1024]{0:T(1024)S(1)} %get-tuple-element.4), kind=kOutput, calls=%fused_computation.16 | convolution fusion | flops 2150629376 | bytes 3149824 | tf_op jit(solution)/shard_map/dot_general | solution.py:28
  36.9 10.5 %all-to-all-start.2 = ((bf16[64,4,8,512]{3,2,1,0:T(8,128)(2,1)}), bf16[64,4,8,512]{3,2,1,0:T(8,128)(2,1)}, u32[]{:S(2)}, u32[]{:S(2)}) async-start(bf16[64,4,8,512]{3,2,1,0:T(8,128)(2,1)} %bitcast.23), calls=%async_computation.2 | async-start | bytes 4194304 | tf_op jit(solution)/shard_map/all_to_all | solution.py:35
  47.5 0.7 reshape.70
  48.2 50.3 %all-to-all-done.2 = bf16[64,4,8,512]{3,2,1,0:T(8,128)(2,1)} async-done(((bf16[64,4,8,512]{3,2,1,0:T(8,128)(2,1)}), bf16[64,4,8,512]{3,2,1,0:T(8,128)(2,1)}, u32[]{:S(2)}, u32[]{:S(2)}) %all-to-all-start.2) | async-done | bytes 2097184 | tf_op jit(solution)/shard_map/all_to_all | solution.py:35
  98.5 4.2 %all-to-all-start.1 = ((s32[4,1,512]{2,1,0:T(1,128)}), s32[4,1,512]{2,1,0:T(1,128)S(1)}, u32[]{:S(2)}, u32[]{:S(2)}) async-start(s32[4,1,512]{2,1,0:T(1,128)} %reshape.70), calls=%async_computation.1 | async-start | bytes 16384 | tf_op jit(solution)/shard_map/all_to_all | solution.py:40
  102.7 3.1 %copy.40 = bf16[64,4,8,512]{3,2,0,1:T(8,128)(2,1)} copy(bf16[64,4,8,512]{3,2,1,0:T(8,128)(2,1)} %all-to-all-done.2) | data formatting | bytes 4194304 | tf_op jit(solution)/shard_map/all_to_all | solution.py:35
  105.8 1.1 all-to-all-done.1
  106.9 4.6 %all-to-all-start.3 = ((bf16[64,4,8,512]{3,2,0,1:T(8,128)(2,1)}), bf16[64,4,8,512]{3,2,0,1:T(8,128)(2,1)}, u32[]{:S(2)}, u32[]{:S(2)}) async-start(bf16[64,4,8,512]{3,2,0,1:T(8,128)(2,1)} %copy.40), calls=%async_computation.3 | async-start | bytes 4194304 | tf_op jit(solution)/shard_map/all_to_all | solution.py:39
  111.5 0.5 broadcast.64
  112.0 0.7 reduce
  113.1 1.0 convert_reduce_fusion
  114.1 21.9 %all-to-all-done.3 = bf16[64,4,8,512]{3,2,0,1:T(8,128)(2,1)} async-done(((bf16[64,4,8,512]{3,2,0,1:T(8,128)(2,1)}), bf16[64,4,8,512]{3,2,0,1:T(8,128)(2,1)}, u32[]{:S(2)}, u32[]{:S(2)}) %all-to-all-start.3) | async-done | bytes 2097184 | tf_op jit(solution)/shard_map/all_to_all | solution.py:39
  136.0 2.0 copy.41
  138.2 3.0 %add_divide_fusion = f32[1024,512]{1,0:T(8,128)S(1)} fusion(f32[1024,512]{1,0:T(8,128)S(1)} %copy-done.5, bf16[2048,512]{1,0:T(8,128)(2,1)S(1)} %bitcast.24, s32[2048]{0:T(1024)S(1)} %sub.27, f32[1024]{0:T(1024)S(1)} %multiply_add_fusion), kind=kOutput, calls=%fused_computation.18 | convolution fusion | flops 2151677952 | bytes 6303744 | tf_op jit(solution)/shard_map/dot_general | solution.py:47
  141.3 2.6 %fusion.9 = bf16[2048,512]{1,0:T(8,128)(2,1)S(1)} fusion(s32[2048]{0:T(1024)S(1)} %sub.27, f32[1024,512]{1,0:T(8,128)S(1)} %add_divide_fusion), kind=kOutput, calls=%fused_computation.15 | convolution fusion | flops 2151153664 | bytes 4202496 | tf_op jit(solution)/shard_map/dot_general | solution.py:53
  143.9 59.2 %all_to_all.30 = bf16[64,4,8,512]{3,2,1,0:T(8,128)(2,1)S(1)} all-to-all(bf16[64,4,8,512]{3,2,1,0:T(8,128)(2,1)S(1)} %bitcast.25), channel_id=1, replica_groups=mesh['hst'=64,'local'=4] {'hst'}, dimensions={0} | all-to-all | bytes 4194304 | tf_op jit(solution)/shard_map/all_to_all | solution.py:58
  203.1 1.5 copy.42
  204.6 4.4 %all-to-all-start.5 = ((bf16[64,4,8,512]{3,2,0,1:T(8,128)(2,1)}), bf16[64,4,8,512]{3,2,0,1:T(8,128)(2,1)}, u32[]{:S(2)}, u32[]{:S(2)}) async-start(bf16[64,4,8,512]{3,2,0,1:T(8,128)(2,1)} %copy.42), calls=%async_computation.5 | async-start | bytes 4194304 | tf_op jit(solution)/shard_map/all_to_all | solution.py:57
  209.1 26.1 %all-to-all-done.5 = bf16[64,4,8,512]{3,2,0,1:T(8,128)(2,1)} async-done(((bf16[64,4,8,512]{3,2,0,1:T(8,128)(2,1)}), bf16[64,4,8,512]{3,2,0,1:T(8,128)(2,1)}, u32[]{:S(2)}, u32[]{:S(2)}) %all-to-all-start.5) | async-done | bytes 2097184 | tf_op jit(solution)/shard_map/all_to_all | solution.py:57
  235.1 3.2 %copy.43 = bf16[64,4,8,512]{3,2,1,0:T(8,128)(2,1)} copy(bf16[64,4,8,512]{3,2,0,1:T(8,128)(2,1)} %all-to-all-done.5) | data formatting | bytes 4194304 | tf_op jit(solution)/shard_map/all_to_all | solution.py:57
  238.4 7.0 %gather_fusion = bf16[1024,512]{1,0:T(8,128)(2,1)} fusion(bf16[2048,512]{1,0:T(8,128)(2,1)} %bitcast.22, s32[1024]{0:T(1024)S(1)} %fusion.20), kind=kCustom, calls=%fused_computation | custom fusion | bytes 2101248 | tf_op jit(solution)/shard_map/jit(_take)/gather | solution.py:65
  245.3 2.4 broadcast_select_fusion
  (30 shorter events, 0.8 us)
Async XLA Ops:
  0.6 19.3 %copy-start = (bf16[3072,512]{1,0:T(8,128)(2,1)S(1)}, bf16[3072,512]{1,0:T(8,128)(2,1)}, u32[]{:S(2)}) copy-start(bf16[3072,512]{1,0:T(8,128)(2,1)} %param.11) | copy-start | bytes 9437188
  1.8 1.0 copy-start.1
  4.1 0.8 copy-start.2
  4.1 15.8 %copy-start.6 = (f32[3072]{0:T(1024)S(1)}, f32[3072]{0:T(1024)}, u32[]{:S(2)}) copy-start(f32[3072]{0:T(1024)} %param.10) | copy-start | bytes 36868
  4.1 15.8 %copy-start.7 = (f32[512]{0:T(512)S(1)}, f32[512]{0:T(512)}, u32[]{:S(2)}) copy-start(f32[512]{0:T(512)} %param.12) | copy-start | bytes 6148
  6.9 30.0 %all-to-all-start = ((s32[64,4,8]{2,1,0:T(4,128)}), s32[64,4,8]{2,1,0:T(4,128)S(1)}, u32[]{:S(2)}, u32[]{:S(2)}) async-start(s32[64,4,8]{2,1,0:T(4,128)} %reshape.56), calls=%async_computation | async-start | bytes 262144 | tf_op jit(solution)/shard_map/all_to_all | solution.py:36
  36.9 61.6 %all-to-all-start.2 = ((bf16[64,4,8,512]{3,2,1,0:T(8,128)(2,1)}), bf16[64,4,8,512]{3,2,1,0:T(8,128)(2,1)}, u32[]{:S(2)}, u32[]{:S(2)}) async-start(bf16[64,4,8,512]{3,2,1,0:T(8,128)(2,1)} %bitcast.23), calls=%async_computation.2 | async-start | bytes 4194304 | tf_op jit(solution)/shard_map/all_to_all | solution.py:35
  98.5 8.4 %all-to-all-start.1 = ((s32[4,1,512]{2,1,0:T(1,128)}), s32[4,1,512]{2,1,0:T(1,128)S(1)}, u32[]{:S(2)}, u32[]{:S(2)}) async-start(s32[4,1,512]{2,1,0:T(1,128)} %reshape.70), calls=%async_computation.1 | async-start | bytes 16384 | tf_op jit(solution)/shard_map/all_to_all | solution.py:40
  105.8 8.2 %copy-start.3 = (f32[1024]{0:T(1024)S(1)}, f32[1024]{0:T(1024)}, u32[]{:S(2)}) copy-start(f32[1024]{0:T(1024)} %param.14) | copy-start | bytes 12292
  106.9 29.1 %all-to-all-start.3 = ((bf16[64,4,8,512]{3,2,0,1:T(8,128)(2,1)}), bf16[64,4,8,512]{3,2,0,1:T(8,128)(2,1)}, u32[]{:S(2)}, u32[]{:S(2)}) async-start(bf16[64,4,8,512]{3,2,0,1:T(8,128)(2,1)} %copy.40), calls=%async_computation.3 | async-start | bytes 4194304 | tf_op jit(solution)/shard_map/all_to_all | solution.py:39
  114.1 24.0 %copy-start.4 = (f32[1024]{0:T(1024)}, f32[1024]{0:T(1024)S(1)}, u32[]{:S(2)}) copy-start(f32[1024]{0:T(1024)S(1)} %multiply_add_fusion) | copy-start | bytes 12292
  136.0 2.2 copy-start.5
  141.3 2.6 %copy-start.8 = (f32[1024,512]{1,0:T(8,128)}, f32[1024,512]{1,0:T(8,128)S(1)}, u32[]{:S(2)}) copy-start(f32[1024,512]{1,0:T(8,128)S(1)} %add_divide_fusion) | copy-start | bytes 6291460
  204.6 30.5 %all-to-all-start.5 = ((bf16[64,4,8,512]{3,2,0,1:T(8,128)(2,1)}), bf16[64,4,8,512]{3,2,0,1:T(8,128)(2,1)}, u32[]{:S(2)}, u32[]{:S(2)}) async-start(bf16[64,4,8,512]{3,2,0,1:T(8,128)(2,1)} %copy.42), calls=%async_computation.5 | async-start | bytes 4194304 | tf_op jit(solution)/shard_map/all_to_all | solution.py:57
where the time goes:
time: 248 us
  waiting for transfers between devices  99.4 us (40%)
  blocking collectives  59.2 us (24%)
  starting transfers between devices  36.7 us (15%)
  matrix products  22.6 us (9%)
  local copies, waits for them, and re-layouts  20.9 us (8%)
  other arithmetic  8.01 us (3%)
    all_to_all x1, blocking collectives, per_device(): lax.all_to_all(replies, 'hst', split_axis=0, concat_axis=0, tiled=True)  59.2 us
    all_to_all x1, waiting for transfers between devices, per_device(): lax.all_to_all(outgoing, 'hst', split_axis=0, concat_axis=0, tiled=True)  50.3 us
    all_to_all x1, waiting for transfers between devices, per_device(): lax.all_to_all(lax.all_to_all(replies, 'hst', split_axis=0, concat_axis=0...  26.1 us
    all_to_all x1, waiting for transfers between devices, per_device(): lax.all_to_all(halfway[0], 'local', split_axis=1, concat_axis=1, tiled=True)  21.9 us
    all_to_all x1, starting transfers between devices, per_device(): lax.all_to_all(sent_ids, 'hst', split_axis=0, concat_axis=0, tiled=True)  13 us
    dot_general x1, matrix products, per_device(): jnp.dot(hidden, w_out, preferred_element_type=jnp.float32) + b_out  12.1 us
    all_to_all x1, starting transfers between devices, per_device(): lax.all_to_all(outgoing, 'hst', split_axis=0, concat_axis=0, tiled=True)  10.5 us
    gather x1, local copies, waits for them, and re-layouts, per_device(): quantized = jnp.take(back_rows, slot_index, axis=0)  6.98 us
  transfers between devices with their start and end apart: 5, of which 4 were waited for; matrix products, arithmetic and copies ran while one was open for 9% of the time, Pallas kernels for 0%

commit v1 on v0

v1 whole, which is shorter than its diff:
```python
import jax
import jax.numpy as jnp
from jax import lax
from jax.sharding import PartitionSpec as P

DECAY = 0.9
AXES = ("hst", "local")
EXTRA = 128


def per_device(patches, w_in, b_in, w_out, b_out, ema_sums, ema_counts, code_ids):
    owner_count = lax.axis_size(AXES)
    code_span = ema_sums.shape[0]
    latent_width = ema_sums.shape[1]
    row_count = patches.shape[0]
    capacity = max(2, 2 * row_count // owner_count)
    slot_count = owner_count * capacity

    pre_act = jnp.dot(patches, w_in, preferred_element_type=jnp.float32) + b_in
    hidden = jnp.tanh(pre_act).astype(jnp.bfloat16)
    latents = (jnp.dot(hidden, w_out, preferred_element_type=jnp.float32) + b_out).astype(
        jnp.bfloat16
    )

    owner_of = code_ids // code_span
    offset = code_ids - owner_of * code_span
    rows = jnp.arange(row_count)
    same = (owner_of[:, None] == owner_of[None, :]) & (rows[None, :] < rows[:, None])
    position = jnp.sum(same.astype(jnp.int32), axis=1)
    slot_index = owner_of * capacity + position
    placing_t = (slot_index[:, None] == jnp.arange(slot_count)[None, :]).astype(jnp.bfloat16)

    lane = jnp.arange(EXTRA)[None, :]
    hi = (offset // 32 + 1).astype(jnp.float32)[:, None]
    lo = (offset % 32).astype(jnp.float32)[:, None]
    extra = jnp.where(lane == 0, 1.0, jnp.where(lane == 1, hi, jnp.where(lane == 2, lo, 0.0)))
    payload = jnp.concatenate([latents, extra.astype(jnp.bfloat16)], axis=1)
    outgoing = lax.dot_general(
        placing_t, payload, (((0,), (0,)), ((), ())), preferred_element_type=jnp.float32
    ).astype(jnp.bfloat16)
    outgoing = outgoing.reshape(owner_count, capacity, latent_width + EXTRA)
    arrived = lax.all_to_all(outgoing, AXES, 0, 0, tiled=True)
    arrived = arrived.reshape(slot_count, latent_width + EXTRA)

    got_hi = arrived[:, latent_width + 1].astype(jnp.int32)
    got_lo = arrived[:, latent_width + 2].astype(jnp.int32)
    got_offset = (got_hi - 1) * 32 + got_lo
    chosen = (got_offset[:, None] == jnp.arange(code_span)[None, :]).astype(jnp.bfloat16)
    totals = lax.dot_general(
        chosen, arrived, (((0,), (0,)), ((), ())), preferred_element_type=jnp.float32
    )
    code_sums = totals[:, :latent_width]
    code_counts = totals[:, latent_width]
    new_counts = DECAY * ema_counts + (1.0 - DECAY) * code_counts
    codebook = (DECAY * ema_sums + (1.0 - DECAY) * code_sums) / new_counts[:, None]
    replies = jnp.dot(
        chosen, codebook.astype(jnp.bfloat16), preferred_element_type=jnp.float32
    ).astype(jnp.bfloat16)
    replies = replies.reshape(owner_count, capacity, latent_width)
    returned = lax.all_to_all(replies, AXES, 0, 0, tiled=True)
    returned = returned.reshape(slot_count, latent_width)
    quantized = jnp.dot(placing_t, returned, preferred_element_type=jnp.float32).astype(
        jnp.bfloat16
    )
    return (codebook, new_counts, quantized)


def solution(mesh):
    in_specs = (
        P(AXES, None),
        P(),
        P(),
        P(),
        P(),
        P(AXES, None),
        P(AXES),
        P(AXES),
    )
    out_specs = (P(AXES, None), P(AXES), P(AXES, None))
    return jax.shard_map(
        per_device, mesh=mesh, in_specs=in_specs, out_specs=out_specs, check_vma=False
    )
```

time: 248 us -> 186 us (0.75)
  blocking collectives: 59.2 us -> 0 us
  waiting for transfers between devices: 99.4 us -> 113 us
  starting transfers between devices: 36.7 us -> 24.3 us
  matrix products: 22.6 us -> 32.2 us
  local copies, waits for them, and re-layouts: 20.9 us -> 12.4 us
  other arithmetic: 8.01 us -> 2.78 us
    all_to_all x1 -> x0, blocking collectives: 59.2 us -> none  [per_device(): lax.all_to_all(replies, 'hst', split_axis=0, concat_axis=0, tiled=True)]
    all_to_all x5 -> x2, waiting for transfers between devices: 99.4 us -> 113 us  [the longest x1 62.1 us: per_device(): arrived = lax.all_to_all(outgoing, AXES, 0, 0, tiled=True)]
    all_to_all x5 -> x2, starting transfers between devices: 36.7 us -> 24.3 us  [the longest x1 16.5 us: per_device(): arrived = lax.all_to_all(outgoing, AXES, 0, 0, tiled=True)]
    all_to_all x6 -> x0, local copies, waits for them, and re-layouts: 10.4 us -> none  [the longest x1 3.21 us: per_device(): lax.all_to_all(lax.all_to_all(replies, 'hst', split_axis=0, concat_axis=0...]
    unnamed x20 -> x14, local copies, waits for them, and re-layouts: 1.96 us -> 9.71 us
    gather x1 -> x0, local copies, waits for them, and re-layouts: 6.98 us -> none  [per_device(): quantized = jnp.take(back_rows, slot_index, axis=0)]
    dot_general x1 -> x2, matrix products: 4.89 us -> 11.3 us  [the longest x1 6.4 us: per_device(): lax.dot_general(placing_t, payload, (((0,), (0,)), ((), ())), preferred_e...]
    slice x0 -> x1, local copies, waits for them, and re-layouts: none -> 2.65 us  [per_device(): got_hi = arrived[:, latent_width + 1].astype(jnp.int32)]
  transfers between devices with their start and end apart: 5 -> 2, of which waited for: 4 -> 2; matrix products, arithmetic and copies ran while one was open for 9% -> 3% of each run, Pallas kernels for 0% -> 0%
where the time goes in v1:
time: 186 us
  waiting for transfers between devices  113 us (61%)
  matrix products  32.2 us (17%)
  starting transfers between devices  24.3 us (13%)
  local copies, waits for them, and re-layouts  12.4 us (7%)
  other arithmetic  2.78 us (1%)
    all_to_all x1, waiting for transfers between devices, per_device(): arrived = lax.all_to_all(outgoing, AXES, 0, 0, tiled=True)  62.1 us
    all_to_all x1, waiting for transfers between devices, per_device(): returned = lax.all_to_all(replies, AXES, 0, 0, tiled=True)  51.2 us
    all_to_all x1, starting transfers between devices, per_device(): arrived = lax.all_to_all(outgoing, AXES, 0, 0, tiled=True)  16.5 us
    dot_general x1, matrix products, per_device(): jnp.dot(hidden, w_out, preferred_element_type=jnp.float32) + b_out  12.1 us
    unnamed x14, local copies, waits for them, and re-layouts  9.71 us
    all_to_all x1, starting transfers between devices, per_device(): returned = lax.all_to_all(replies, AXES, 0, 0, tiled=True)  7.77 us
    dot_general x1, matrix products, per_device(): lax.dot_general(placing_t, payload, (((0,), (0,)), ((), ())), preferred_e...  6.4 us
    dot_general x1, matrix products, per_device(): lax.dot_general(chosen, arrived, (((0,), (0,)), ((), ())), preferred_elem...  5.15 us
  transfers between devices with their start and end apart: 2, of which 2 were waited for; matrix products, arithmetic and copies ran while one was open for 3% of the time, Pallas kernels for 0%

profile of v1, /device:TPU:1, one launch (start us, length us, event | category | flops | bytes accessed | tf_op | source)
XLA Modules:
  0.0 185.7 jit_solution(5954753518313690364)
XLA Ops:
  0.6 0.0 copy-start
  0.7 0.8 add_select_fusion.2
  1.5 0.5 convert_reduce_fusion
  2.0 0.7 fusion.35
  2.8 0.2 select_convert_fusion
  2.9 0.0 copy-done
  2.9 12.1 %add_convert_fusion = bf16[1024,512]{0,1:T(8,128)(2,1)} fusion(bf16[3072,512]{1,0:T(8,128)(2,1)S(1)} %copy-done, f32[3072]{0:T(1024)} %param.10, bf16[1024,768]{1,0:T(8,128)(2,1)} %param.8, bf16[768,3072]{1,0:T(8,128)(2,1)} %param.9, f32[512]{0:T(512)} %param.12), kind=kOutput, calls=%fused_computation.24 | convolution fusion | flops 8060403712 | bytes 10500096 | tf_op jit(solution)/shard_map/dot_general | solution.py:21
  15.0 6.4 %fusion.22 = bf16[256,8,640]{2,1,0:T(8,128)(2,1)} fusion(s32[1024]{0:T(1024)S(1)} %get-tuple-element.21, bf16[1024,128]{0,1:T(8,128)(2,1)S(1)} %select_convert_fusion, bf16[1024,512]{0,1:T(8,128)(2,1)} %add_convert_fusion), kind=kOutput, calls=%fused_computation.25 | convolution fusion | flops 2692481024 | bytes 3936256 | tf_op jit(solution)/shard_map/dot_general | solution.py:38
  21.4 16.5 %all-to-all-start = ((bf16[256,8,640]{2,1,0:T(8,128)(2,1)}), bf16[256,8,640]{2,1,0:T(8,128)(2,1)}, u32[]{:S(2)}, u32[]{:S(2)}) async-start(bf16[256,8,640]{2,1,0:T(8,128)(2,1)} %fusion.22), calls=%async_computation | async-start | bytes 5242880 | tf_op jit(solution)/shard_map/all_to_all | solution.py:42
  38.0 2.9 %copy.20 = f32[1024,512]{0,1:T(8,128)} copy(f32[1024,512]{1,0:T(8,128)} %param.13) | data formatting | bytes 4194304 | tf_op args[5]
  40.9 62.1 %all-to-all-done = bf16[256,8,640]{2,1,0:T(8,128)(2,1)} async-done(((bf16[256,8,640]{2,1,0:T(8,128)(2,1)}), bf16[256,8,640]{2,1,0:T(8,128)(2,1)}, u32[]{:S(2)}, u32[]{:S(2)}) %all-to-all-start) | async-done | bytes 2621472 | tf_op jit(solution)/shard_map/all_to_all | solution.py:42
  103.0 2.6 %fusion.42 = (bf16[2048,1]{1,0:T(8,128)(2,1)}, bf16[2048,1]{1,0:T(8,128)(2,1)}) fusion(bf16[2048,640]{1,0:T(8,128)(2,1)} %bitcast.1), kind=kLoop, calls=%fused_computation.61 | loop fusion | bytes 16384 | tf_op jit(solution)/shard_map/slice | solution.py:45
  105.6 1.2 copy.24
  106.9 1.3 copy.25
  108.2 0.0 copy-start.4
  108.2 0.0 copy-start.1
  108.2 5.1 %fusion.1 = f32[1024,640]{0,1:T(8,128)S(1)} fusion(s32[2048]{0:T(1024)S(1)} %bitcast.18, bf16[256,8,640]{2,1,0:T(8,128)(2,1)} %all-to-all-done), kind=kOutput, calls=%fused_computation.3 | convolution fusion | flops 2686451712 | bytes 5251072 | tf_op jit(solution)/shard_map/dot_general | solution.py:49
  113.4 0.0 copy-done.4
  113.4 0.0 copy-done.1
  113.4 0.0 copy-start.3
  113.4 0.5 fusion.20
  113.9 0.1 copy-done.3
  114.0 0.0 copy-start.2
  114.0 1.3 copy-done.2
  115.3 3.6 %fusion.25 = bf16[256,8,512]{2,1,0:T(8,128)(2,1)} fusion(s32[2048]{0:T(1024)S(1)} %bitcast.19, f32[1024,512]{0,1:T(8,128)S(1)} %fusion.20), kind=kOutput, calls=%fused_computation.26 | convolution fusion | flops 2151153664 | bytes 4202496 | tf_op jit(solution)/shard_map/dot_general | solution.py:56
  118.9 7.8 %all-to-all-start.1 = ((bf16[256,8,512]{2,1,0:T(8,128)(2,1)}), bf16[256,8,512]{2,1,0:T(8,128)(2,1)}, u32[]{:S(2)}, u32[]{:S(2)}) async-start(bf16[256,8,512]{2,1,0:T(8,128)(2,1)} %fusion.25), calls=%async_computation.1 | async-start | bytes 4194304 | tf_op jit(solution)/shard_map/all_to_all | solution.py:60
  126.7 2.9 %copy.23 = f32[1024,512]{1,0:T(8,128)} copy(f32[1024,512]{0,1:T(8,128)} %copy-done.2) | data formatting | bytes 4194304
  129.6 51.2 %all-to-all-done.1 = bf16[256,8,512]{2,1,0:T(8,128)(2,1)} async-done(((bf16[256,8,512]{2,1,0:T(8,128)(2,1)}), bf16[256,8,512]{2,1,0:T(8,128)(2,1)}, u32[]{:S(2)}, u32[]{:S(2)}) %all-to-all-start.1) | async-done | bytes 2097184 | tf_op jit(solution)/shard_map/all_to_all | solution.py:60
  180.8 4.9 %fusion.26 = bf16[1024,512]{1,0:T(8,128)(2,1)} fusion(bf16[256,8,512]{2,1,0:T(8,128)(2,1)} %all-to-all-done.1, s32[1024]{0:T(1024)S(1)} %get-tuple-element.21), kind=kOutput, calls=%fused_computation.27 | convolution fusion | flops 2150105088 | bytes 3149824 | tf_op jit(solution)/shard_map/dot_general | solution.py:62
  (5 shorter events, 0.1 us)
Async XLA Ops:
  0.6 2.3 %copy-start = (bf16[3072,512]{1,0:T(8,128)(2,1)S(1)}, bf16[3072,512]{1,0:T(8,128)(2,1)}, u32[]{:S(2)}) copy-start(bf16[3072,512]{1,0:T(8,128)(2,1)} %param.11) | copy-start | bytes 9437188
  21.4 81.6 %all-to-all-start = ((bf16[256,8,640]{2,1,0:T(8,128)(2,1)}), bf16[256,8,640]{2,1,0:T(8,128)(2,1)}, u32[]{:S(2)}, u32[]{:S(2)}) async-start(bf16[256,8,640]{2,1,0:T(8,128)(2,1)} %fusion.22), calls=%async_computation | async-start | bytes 5242880 | tf_op jit(solution)/shard_map/all_to_all | solution.py:42
  108.2 5.2 %copy-start.4 = (f32[1024]{0:T(1024)S(1)}, f32[1024]{0:T(1024)}, u32[]{:S(2)}) copy-start(f32[1024]{0:T(1024)} %param.14) | copy-start | bytes 12292
  108.2 5.2 %copy-start.1 = (f32[1024,512]{0,1:T(8,128)S(1)}, f32[1024,512]{0,1:T(8,128)}, u32[]{:S(2)}) copy-start(f32[1024,512]{0,1:T(8,128)} %copy.20) | copy-start | bytes 6291460
  113.4 0.6 copy-start.3
  114.0 1.3 copy-start.2
  118.9 61.8 %all-to-all-start.1 = ((bf16[256,8,512]{2,1,0:T(8,128)(2,1)}), bf16[256,8,512]{2,1,0:T(8,128)(2,1)}, u32[]{:S(2)}, u32[]{:S(2)}) async-start(bf16[256,8,512]{2,1,0:T(8,128)(2,1)} %fusion.25), calls=%async_computation.1 | async-start | bytes 4194304 | tf_op jit(solution)/shard_map/all_to_all | solution.py:60

commit v2 on v1

--- a/solution.py
+++ b/solution.py
@@ -42,9 +42,9 @@
     arrived = lax.all_to_all(outgoing, AXES, 0, 0, tiled=True)
     arrived = arrived.reshape(slot_count, latent_width + EXTRA)
 
-    got_hi = arrived[:, latent_width + 1].astype(jnp.int32)
-    got_lo = arrived[:, latent_width + 2].astype(jnp.int32)
-    got_offset = (got_hi - 1) * 32 + got_lo
+    weight = jnp.where(lane == 1, 32.0, jnp.where(lane == 2, 1.0, 0.0))
+    got_offset = jnp.sum(arrived[:, latent_width:].astype(jnp.float32) * weight, axis=1)
+    got_offset = got_offset.astype(jnp.int32) - 32
     chosen = (got_offset[:, None] == jnp.arange(code_span)[None, :]).astype(jnp.bfloat16)
     totals = lax.dot_general(
         chosen, arrived, (((0,), (0,)), ((), ())), preferred_element_type=jnp.float32

time: 186 us -> 183 us (0.984)
  local copies, waits for them, and re-layouts: 12.4 us -> 7.19 us
    slice x1 -> x0, local copies, waits for them, and re-layouts: 2.65 us -> none  [per_device(): got_hi = arrived[:, latent_width + 1].astype(jnp.int32)]
    unnamed x14 -> x12, local copies, waits for them, and re-layouts: 9.71 us -> 7.19 us
where the time goes in v2:
time: 183 us; the launch traced here: 182 us
  waiting for transfers between devices  113 us (62%)
  matrix products  32.5 us (18%)
  starting transfers between devices  24.3 us (13%)
  local copies, waits for them, and re-layouts  7.19 us (4%)
  other arithmetic  4.32 us (2%)
    all_to_all x1, waiting for transfers between devices, per_device(): arrived = lax.all_to_all(outgoing, AXES, 0, 0, tiled=True)  62.1 us
    all_to_all x1, waiting for transfers between devices, per_device(): returned = lax.all_to_all(replies, AXES, 0, 0, tiled=True)  51.2 us
    all_to_all x1, starting transfers between devices, per_device(): arrived = lax.all_to_all(outgoing, AXES, 0, 0, tiled=True)  16.5 us
    dot_general x1, matrix products, per_device(): jnp.dot(hidden, w_out, preferred_element_type=jnp.float32) + b_out  12.1 us
    all_to_all x1, starting transfers between devices, per_device(): returned = lax.all_to_all(replies, AXES, 0, 0, tiled=True)  7.76 us
    unnamed x12, local copies, waits for them, and re-layouts  7.19 us
    dot_general x1, matrix products, per_device(): lax.dot_general(placing_t, payload, (((0,), (0,)), ((), ())), preferred_e...  6.67 us
    dot_general x1, matrix products, per_device(): lax.dot_general(chosen, arrived, (((0,), (0,)), ((), ())), preferred_elem...  5.15 us
  transfers between devices with their start and end apart: 2, of which 2 were waited for; matrix products, arithmetic and copies ran while one was open for 3% of the time, Pallas kernels for 0%

profile of v2, /device:TPU:1, one launch (start us, length us, event | category | flops | bytes accessed | tf_op | source)
XLA Modules:
  0.0 182.3 jit_solution(7746835103756565571)
XLA Ops:
  0.6 0.0 copy-start
  0.7 0.8 add_select_fusion.2
  1.5 0.5 convert_reduce_fusion
  2.0 0.7 fusion.29
  2.8 0.3 select_convert_fusion
  3.1 0.0 copy-done
  3.1 12.1 %add_convert_fusion = bf16[1024,512]{1,0:T(8,128)(2,1)} fusion(bf16[3072,512]{1,0:T(8,128)(2,1)S(1)} %copy-done, f32[3072]{0:T(1024)} %param.10, bf16[1024,768]{1,0:T(8,128)(2,1)} %param.8, bf16[768,3072]{1,0:T(8,128)(2,1)} %param.9, f32[512]{0:T(512)} %param.12), kind=kOutput, calls=%fused_computation.23 | convolution fusion | flops 8060403712 | bytes 10500096 | tf_op jit(solution)/shard_map/dot_general | solution.py:21
  15.2 6.7 %fusion.18 = bf16[256,8,640]{2,1,0:T(8,128)(2,1)} fusion(s32[1024]{0:T(1024)S(1)} %get-tuple-element.10, bf16[1024,128]{1,0:T(8,128)(2,1)S(1)} %select_convert_fusion, bf16[1024,512]{1,0:T(8,128)(2,1)} %add_convert_fusion), kind=kOutput, calls=%fused_computation.24 | convolution fusion | flops 2690383872 | bytes 3936256 | tf_op jit(solution)/shard_map/dot_general | solution.py:38
  21.9 16.5 %all-to-all-start = ((bf16[256,8,640]{2,1,0:T(8,128)(2,1)}), bf16[256,8,640]{2,1,0:T(8,128)(2,1)}, u32[]{:S(2)}, u32[]{:S(2)}) async-start(bf16[256,8,640]{2,1,0:T(8,128)(2,1)} %fusion.18), calls=%async_computation | async-start | bytes 5242880 | tf_op jit(solution)/shard_map/all_to_all | solution.py:42
  38.4 2.9 %copy.13 = f32[1024,512]{0,1:T(8,128)} copy(f32[1024,512]{1,0:T(8,128)} %param.13) | data formatting | bytes 4194304 | tf_op args[5]
  41.3 62.1 %all-to-all-done = bf16[256,8,640]{2,1,0:T(8,128)(2,1)} async-done(((bf16[256,8,640]{2,1,0:T(8,128)(2,1)}), bf16[256,8,640]{2,1,0:T(8,128)(2,1)}, u32[]{:S(2)}, u32[]{:S(2)}) %all-to-all-start) | async-done | bytes 2621472 | tf_op jit(solution)/shard_map/all_to_all | solution.py:42
  103.4 1.4 multiply_reduce_fusion
  104.8 0.0 copy-start.4
  104.9 0.0 copy-start.1
  104.9 5.1 %fusion.1 = f32[1024,640]{0,1:T(8,128)S(1)} fusion(s32[2048]{0:T(1024)S(1)} %convert_add_fusion, bf16[256,8,640]{2,1,0:T(8,128)(2,1)} %all-to-all-done), kind=kOutput, calls=%fused_computation.3 | convolution fusion | flops 2686451712 | bytes 5251072 | tf_op jit(solution)/shard_map/dot_general | solution.py:49
  110.0 0.0 copy-done.4
  110.1 0.0 copy-done.1
  110.1 0.0 copy-start.3
  110.1 0.5 fusion.16
  110.6 0.1 copy-done.3
  110.7 0.0 copy-start.2
  110.7 1.3 copy-done.2
  112.0 3.6 %fusion.19 = bf16[256,8,512]{2,1,0:T(8,128)(2,1)} fusion(s32[2048]{0:T(1024)S(1)} %convert_add_fusion, f32[1024,512]{0,1:T(8,128)S(1)} %fusion.16), kind=kOutput, calls=%fused_computation.25 | convolution fusion | flops 2151153664 | bytes 4202496 | tf_op jit(solution)/shard_map/dot_general | solution.py:56
  115.6 7.8 %all-to-all-start.1 = ((bf16[256,8,512]{2,1,0:T(8,128)(2,1)}), bf16[256,8,512]{2,1,0:T(8,128)(2,1)}, u32[]{:S(2)}, u32[]{:S(2)}) async-start(bf16[256,8,512]{2,1,0:T(8,128)(2,1)} %fusion.19), calls=%async_computation.1 | async-start | bytes 4194304 | tf_op jit(solution)/shard_map/all_to_all | solution.py:60
  123.3 2.9 %copy.14 = f32[1024,512]{1,0:T(8,128)} copy(f32[1024,512]{0,1:T(8,128)} %copy-done.2) | data formatting | bytes 4194304
  126.2 51.2 %all-to-all-done.1 = bf16[256,8,512]{2,1,0:T(8,128)(2,1)} async-done(((bf16[256,8,512]{2,1,0:T(8,128)(2,1)}), bf16[256,8,512]{2,1,0:T(8,128)(2,1)}, u32[]{:S(2)}, u32[]{:S(2)}) %all-to-all-start.1) | async-done | bytes 2097184 | tf_op jit(solution)/shard_map/all_to_all | solution.py:60
  177.4 4.9 %fusion.20 = bf16[1024,512]{1,0:T(8,128)(2,1)} fusion(bf16[256,8,512]{2,1,0:T(8,128)(2,1)} %all-to-all-done.1, s32[1024]{0:T(1024)S(1)} %get-tuple-element.10), kind=kOutput, calls=%fused_computation.26 | convolution fusion | flops 2150105088 | bytes 3149824 | tf_op jit(solution)/shard_map/dot_general | solution.py:62
  (6 shorter events, 0.0 us)
Async XLA Ops:
  0.6 2.5 %copy-start = (bf16[3072,512]{1,0:T(8,128)(2,1)S(1)}, bf16[3072,512]{1,0:T(8,128)(2,1)}, u32[]{:S(2)}) copy-start(bf16[3072,512]{1,0:T(8,128)(2,1)} %param.11) | copy-start | bytes 9437188
  21.9 81.6 %all-to-all-start = ((bf16[256,8,640]{2,1,0:T(8,128)(2,1)}), bf16[256,8,640]{2,1,0:T(8,128)(2,1)}, u32[]{:S(2)}, u32[]{:S(2)}) async-start(bf16[256,8,640]{2,1,0:T(8,128)(2,1)} %fusion.18), calls=%async_computation | async-start | bytes 5242880 | tf_op jit(solution)/shard_map/all_to_all | solution.py:42
  104.8 5.2 %copy-start.4 = (f32[1024]{0:T(1024)S(1)}, f32[1024]{0:T(1024)}, u32[]{:S(2)}) copy-start(f32[1024]{0:T(1024)} %param.14) | copy-start | bytes 12292
  104.9 5.2 %copy-start.1 = (f32[1024,512]{0,1:T(8,128)S(1)}, f32[1024,512]{0,1:T(8,128)}, u32[]{:S(2)}) copy-start(f32[1024,512]{0,1:T(8,128)} %copy.13) | copy-start | bytes 6291460
  110.1 0.6 copy-start.3
  110.7 1.3 copy-start.2
  115.6 61.8 %all-to-all-start.1 = ((bf16[256,8,512]{2,1,0:T(8,128)(2,1)}), bf16[256,8,512]{2,1,0:T(8,128)(2,1)}, u32[]{:S(2)}, u32[]{:S(2)}) async-start(bf16[256,8,512]{2,1,0:T(8,128)(2,1)} %fusion.19), calls=%async_computation.1 | async-start | bytes 4194304 | tf_op jit(solution)/shard_map/all_to_all | solution.py:60

commit v3 on v2

--- a/solution.py
+++ b/solution.py
@@ -27,7 +27,10 @@
     rows = jnp.arange(row_count)
     same = (owner_of[:, None] == owner_of[None, :]) & (rows[None, :] < rows[:, None])
     position = jnp.sum(same.astype(jnp.int32), axis=1)
-    slot_index = owner_of * capacity + position
+    local_count = lax.axis_size("local")
+    host_count = owner_count // local_count
+    chunk = (owner_of % local_count) * host_count + owner_of // local_count
+    slot_index = chunk * capacity + position
     placing_t = (slot_index[:, None] == jnp.arange(slot_count)[None, :]).astype(jnp.bfloat16)
 
     lane = jnp.arange(EXTRA)[None, :]
@@ -39,7 +42,7 @@
         placing_t, payload, (((0,), (0,)), ((), ())), preferred_element_type=jnp.float32
     ).astype(jnp.bfloat16)
     outgoing = outgoing.reshape(owner_count, capacity, latent_width + EXTRA)
-    arrived = lax.all_to_all(outgoing, AXES, 0, 0, tiled=True)
+    arrived = lax.all_to_all(outgoing, ("local", "hst"), 0, 0, tiled=True)
     arrived = arrived.reshape(slot_count, latent_width + EXTRA)
 
     weight = jnp.where(lane == 1, 32.0, jnp.where(lane == 2, 1.0, 0.0))
@@ -57,7 +60,7 @@
         chosen, codebook.astype(jnp.bfloat16), preferred_element_type=jnp.float32
     ).astype(jnp.bfloat16)
     replies = replies.reshape(owner_count, capacity, latent_width)
-    returned = lax.all_to_all(replies, AXES, 0, 0, tiled=True)
+    returned = lax.all_to_all(replies, ("local", "hst"), 0, 0, tiled=True)
     returned = returned.reshape(slot_count, latent_width)
     quantized = jnp.dot(placing_t, returned, preferred_element_type=jnp.float32).astype(
         jnp.bfloat16

time: 183 us -> 181 us (0.989)
  no operation moved by 1% of the time
where the time goes in v3:
time: 181 us; the launch traced here: 180 us
  waiting for transfers between devices  112 us (62%)
  matrix products  32.5 us (18%)
  starting transfers between devices  23.4 us (13%)
  local copies, waits for them, and re-layouts  7.19 us (4%)
  other arithmetic  4.32 us (2%)
    all_to_all x1, waiting for transfers between devices, per_device(): arrived = lax.all_to_all(outgoing, ('local', 'hst'), 0, 0, tiled=True)  62.4 us
    all_to_all x1, waiting for transfers between devices, per_device(): returned = lax.all_to_all(replies, ('local', 'hst'), 0, 0, tiled=True)  49.7 us
    all_to_all x1, starting transfers between devices, per_device(): arrived = lax.all_to_all(outgoing, ('local', 'hst'), 0, 0, tiled=True)  16.5 us
    dot_general x1, matrix products, per_device(): jnp.dot(hidden, w_out, preferred_element_type=jnp.float32) + b_out  12.1 us
    unnamed x12, local copies, waits for them, and re-layouts  7.19 us
    all_to_all x1, starting transfers between devices, per_device(): returned = lax.all_to_all(replies, ('local', 'hst'), 0, 0, tiled=True)  6.85 us
    dot_general x1, matrix products, per_device(): lax.dot_general(placing_t, payload, (((0,), (0,)), ((), ())), preferred_e...  6.67 us
    dot_general x1, matrix products, per_device(): lax.dot_general(chosen, arrived, (((0,), (0,)), ((), ())), preferred_elem...  5.15 us
  transfers between devices with their start and end apart: 2, of which 2 were waited for; matrix products, arithmetic and copies ran while one was open for 3% of the time, Pallas kernels for 0%

profile of v3, /device:TPU:1, one launch (start us, length us, event | category | flops | bytes accessed | tf_op | source)
XLA Modules:
  0.0 180.2 jit_solution(12952082666089611933)
XLA Ops:
  0.6 0.0 copy-start
  0.7 0.8 add_select_fusion.4
  1.5 0.5 convert_reduce_fusion
  2.0 0.7 fusion.33
  2.8 0.3 select_convert_fusion
  3.1 0.0 copy-done
  3.1 12.1 %add_convert_fusion = bf16[1024,512]{1,0:T(8,128)(2,1)} fusion(bf16[3072,512]{1,0:T(8,128)(2,1)S(1)} %copy-done, f32[3072]{0:T(1024)} %param.10, bf16[1024,768]{1,0:T(8,128)(2,1)} %param.8, bf16[768,3072]{1,0:T(8,128)(2,1)} %param.9, f32[512]{0:T(512)} %param.12), kind=kOutput, calls=%fused_computation.23 | convolution fusion | flops 8060403712 | bytes 10500096 | tf_op jit(solution)/shard_map/dot_general | solution.py:21
  15.2 6.7 %fusion.18 = bf16[256,8,640]{2,1,0:T(8,128)(2,1)} fusion(s32[1024]{0:T(1024)S(1)} %get-tuple-element.10, bf16[1024,128]{1,0:T(8,128)(2,1)S(1)} %select_convert_fusion, bf16[1024,512]{1,0:T(8,128)(2,1)} %add_convert_fusion), kind=kOutput, calls=%fused_computation.24 | convolution fusion | flops 2690383872 | bytes 3936256 | tf_op jit(solution)/shard_map/dot_general | solution.py:41
  21.9 16.5 %all-to-all-start = ((bf16[256,8,640]{2,1,0:T(8,128)(2,1)}), bf16[256,8,640]{2,1,0:T(8,128)(2,1)}, u32[]{:S(2)}, u32[]{:S(2)}) async-start(bf16[256,8,640]{2,1,0:T(8,128)(2,1)} %fusion.18), calls=%async_computation | async-start | bytes 5242880 | tf_op jit(solution)/shard_map/all_to_all | solution.py:45
  38.4 2.9 %copy.13 = f32[1024,512]{0,1:T(8,128)} copy(f32[1024,512]{1,0:T(8,128)} %param.13) | data formatting | bytes 4194304 | tf_op args[5]
  41.3 62.4 %all-to-all-done = bf16[256,8,640]{2,1,0:T(8,128)(2,1)} async-done(((bf16[256,8,640]{2,1,0:T(8,128)(2,1)}), bf16[256,8,640]{2,1,0:T(8,128)(2,1)}, u32[]{:S(2)}, u32[]{:S(2)}) %all-to-all-start) | async-done | bytes 2621472 | tf_op jit(solution)/shard_map/all_to_all | solution.py:45
  103.7 1.4 multiply_reduce_fusion
  105.1 0.0 copy-start.4
  105.1 0.0 copy-start.1
  105.1 5.2 %fusion.1 = f32[1024,640]{0,1:T(8,128)S(1)} fusion(s32[2048]{0:T(1024)S(1)} %convert_add_fusion, bf16[256,8,640]{2,1,0:T(8,128)(2,1)} %all-to-all-done), kind=kOutput, calls=%fused_computation.3 | convolution fusion | flops 2686451712 | bytes 5251072 | tf_op jit(solution)/shard_map/dot_general | solution.py:52
  110.3 0.0 copy-done.4
  110.3 0.0 copy-done.1
  110.3 0.0 copy-start.3
  110.3 0.5 fusion.16
  110.8 0.1 copy-done.3
  110.9 0.0 copy-start.2
  110.9 1.3 copy-done.2
  112.2 3.6 %fusion.19 = bf16[256,8,512]{2,1,0:T(8,128)(2,1)} fusion(s32[2048]{0:T(1024)S(1)} %convert_add_fusion, f32[1024,512]{0,1:T(8,128)S(1)} %fusion.16), kind=kOutput, calls=%fused_computation.25 | convolution fusion | flops 2151153664 | bytes 4202496 | tf_op jit(solution)/shard_map/dot_general | solution.py:59
  115.8 6.8 %all-to-all-start.1 = ((bf16[256,8,512]{2,1,0:T(8,128)(2,1)}), bf16[256,8,512]{2,1,0:T(8,128)(2,1)}, u32[]{:S(2)}, u32[]{:S(2)}) async-start(bf16[256,8,512]{2,1,0:T(8,128)(2,1)} %fusion.19), calls=%async_computation.1 | async-start | bytes 4194304 | tf_op jit(solution)/shard_map/all_to_all | solution.py:63
  122.7 2.9 %copy.14 = f32[1024,512]{1,0:T(8,128)} copy(f32[1024,512]{0,1:T(8,128)} %copy-done.2) | data formatting | bytes 4194304
  125.6 49.7 %all-to-all-done.1 = bf16[256,8,512]{2,1,0:T(8,128)(2,1)} async-done(((bf16[256,8,512]{2,1,0:T(8,128)(2,1)}), bf16[256,8,512]{2,1,0:T(8,128)(2,1)}, u32[]{:S(2)}, u32[]{:S(2)}) %all-to-all-start.1) | async-done | bytes 2097184 | tf_op jit(solution)/shard_map/all_to_all | solution.py:63
  175.3 4.9 %fusion.20 = bf16[1024,512]{1,0:T(8,128)(2,1)} fusion(bf16[256,8,512]{2,1,0:T(8,128)(2,1)} %all-to-all-done.1, s32[1024]{0:T(1024)S(1)} %get-tuple-element.10), kind=kOutput, calls=%fused_computation.26 | convolution fusion | flops 2150105088 | bytes 3149824 | tf_op jit(solution)/shard_map/dot_general | solution.py:65
  (6 shorter events, 0.0 us)
Async XLA Ops:
  0.6 2.5 %copy-start = (bf16[3072,512]{1,0:T(8,128)(2,1)S(1)}, bf16[3072,512]{1,0:T(8,128)(2,1)}, u32[]{:S(2)}) copy-start(bf16[3072,512]{1,0:T(8,128)(2,1)} %param.11) | copy-start | bytes 9437188
  21.9 81.8 %all-to-all-start = ((bf16[256,8,640]{2,1,0:T(8,128)(2,1)}), bf16[256,8,640]{2,1,0:T(8,128)(2,1)}, u32[]{:S(2)}, u32[]{:S(2)}) async-start(bf16[256,8,640]{2,1,0:T(8,128)(2,1)} %fusion.18), calls=%async_computation | async-start | bytes 5242880 | tf_op jit(solution)/shard_map/all_to_all | solution.py:45
  105.1 5.2 %copy-start.4 = (f32[1024]{0:T(1024)S(1)}, f32[1024]{0:T(1024)}, u32[]{:S(2)}) copy-start(f32[1024]{0:T(1024)} %param.14) | copy-start | bytes 12292
  105.1 5.2 %copy-start.1 = (f32[1024,512]{0,1:T(8,128)S(1)}, f32[1024,512]{0,1:T(8,128)}, u32[]{:S(2)}) copy-start(f32[1024,512]{0,1:T(8,128)} %copy.13) | copy-start | bytes 6291460
  110.3 0.6 copy-start.3
  110.9 1.3 copy-start.2
  115.8 59.5 %all-to-all-start.1 = ((bf16[256,8,512]{2,1,0:T(8,128)(2,1)}), bf16[256,8,512]{2,1,0:T(8,128)(2,1)}, u32[]{:S(2)}, u32[]{:S(2)}) async-start(bf16[256,8,512]{2,1,0:T(8,128)(2,1)} %fusion.19), calls=%async_computation.1 | async-start | bytes 4194304 | tf_op jit(solution)/shard_map/all_to_all | solution.py:63

commit v4 on v3

--- a/solution.py
+++ b/solution.py
@@ -55,10 +55,18 @@
     code_sums = totals[:, :latent_width]
     code_counts = totals[:, latent_width]
     new_counts = DECAY * ema_counts + (1.0 - DECAY) * code_counts
-    codebook = (DECAY * ema_sums + (1.0 - DECAY) * code_sums) / new_counts[:, None]
+    for_replies = (DECAY * ema_sums + (1.0 - DECAY) * code_sums) / new_counts[:, None]
     replies = jnp.dot(
-        chosen, codebook.astype(jnp.bfloat16), preferred_element_type=jnp.float32
+        chosen, for_replies.astype(jnp.bfloat16), preferred_element_type=jnp.float32
     ).astype(jnp.bfloat16)
+    again, again_offset, again_counts = lax.optimization_barrier((arrived, got_offset, new_counts))
+    again_chosen = (again_offset[:, None] == jnp.arange(code_span)[None, :]).astype(jnp.bfloat16)
+    again_totals = lax.dot_general(
+        again_chosen, again, (((0,), (0,)), ((), ())), preferred_element_type=jnp.float32
+    )
+    codebook = (
+        DECAY * ema_sums + (1.0 - DECAY) * again_totals[:, :latent_width]
+    ) / again_counts[:, None]
     replies = replies.reshape(owner_count, capacity, latent_width)
     returned = lax.all_to_all(replies, ("local", "hst"), 0, 0, tiled=True)
     returned = returned.reshape(slot_count, latent_width)

time: 181 us -> 179 us (0.989)
  matrix products: 32.5 us -> 38.9 us
  waiting for transfers between devices: 112 us -> 106 us
    dot_general x1 -> x2, matrix products: 3.61 us -> 10 us  [the longest x1 6.33 us: per_device(): lax.dot_general(again_chosen, again, (((0,), (0,)), ((), ())), preferred_...]
    all_to_all x1, waiting for transfers between devices: 49.7 us -> 43.4 us  [per_device(): returned = lax.all_to_all(replies, ('local', 'hst'), 0, 0, tiled=True)]
    unnamed x12 -> x10, local copies, waits for them, and re-layouts: 7.19 us -> 5.79 us
  transfers between devices with their start and end apart: 2 -> 2, of which waited for: 2 -> 2; matrix products, arithmetic and copies ran while one was open for 3% -> 7% of each run, Pallas kernels for 0% -> 0%
where the time goes in v4:
time: 179 us; the launch traced here: 178 us
  waiting for transfers between devices  106 us (59%)
  matrix products  38.9 us (22%)
  starting transfers between devices  23.4 us (13%)
  local copies, waits for them, and re-layouts  5.79 us (3%)
  other arithmetic  3.84 us (2%)
    all_to_all x1, waiting for transfers between devices, per_device(): arrived = lax.all_to_all(outgoing, ('local', 'hst'), 0, 0, tiled=True)  62.4 us
    all_to_all x1, waiting for transfers between devices, per_device(): returned = lax.all_to_all(replies, ('local', 'hst'), 0, 0, tiled=True)  43.4 us
    all_to_all x1, starting transfers between devices, per_device(): arrived = lax.all_to_all(outgoing, ('local', 'hst'), 0, 0, tiled=True)  16.5 us
    dot_general x1, matrix products, per_device(): jnp.dot(hidden, w_out, preferred_element_type=jnp.float32) + b_out  12.1 us
    all_to_all x1, starting transfers between devices, per_device(): returned = lax.all_to_all(replies, ('local', 'hst'), 0, 0, tiled=True)  6.85 us
    dot_general x1, matrix products, per_device(): lax.dot_general(placing_t, payload, (((0,), (0,)), ((), ())), preferred_e...  6.68 us
    dot_general x1, matrix products, per_device(): lax.dot_general(again_chosen, again, (((0,), (0,)), ((), ())), preferred_...  6.33 us
    unnamed x10, local copies, waits for them, and re-layouts  5.79 us
  transfers between devices with their start and end apart: 2, of which 2 were waited for; matrix products, arithmetic and copies ran while one was open for 7% of the time, Pallas kernels for 0%

profile of v4, /device:TPU:1, one launch (start us, length us, event | category | flops | bytes accessed | tf_op | source)
XLA Modules:
  0.0 178.4 jit_solution(13295206226002706455)
XLA Ops:
  0.6 0.0 copy-start
  0.7 0.8 add_select_fusion.4
  1.5 0.5 convert_reduce_fusion
  2.0 0.7 fusion.39
  2.8 0.3 select_convert_fusion
  3.1 0.0 copy-done
  3.1 12.1 %add_convert_fusion = bf16[1024,512]{1,0:T(8,128)(2,1)} fusion(bf16[3072,512]{1,0:T(8,128)(2,1)S(1)} %copy-done, f32[3072]{0:T(1024)} %param.10, bf16[1024,768]{1,0:T(8,128)(2,1)} %param.8, bf16[768,3072]{1,0:T(8,128)(2,1)} %param.9, f32[512]{0:T(512)} %param.12), kind=kOutput, calls=%fused_computation.28 | convolution fusion | flops 8060403712 | bytes 10500096 | tf_op jit(solution)/shard_map/dot_general | solution.py:21
  15.2 6.7 %fusion.22 = bf16[256,8,640]{2,1,0:T(8,128)(2,1)} fusion(s32[1024]{0:T(1024)S(1)} %get-tuple-element.16, bf16[1024,128]{1,0:T(8,128)(2,1)S(1)} %select_convert_fusion, bf16[1024,512]{1,0:T(8,128)(2,1)} %add_convert_fusion), kind=kOutput, calls=%fused_computation.30 | convolution fusion | flops 2690383872 | bytes 3936256 | tf_op jit(solution)/shard_map/dot_general | solution.py:41
  21.9 16.5 %all-to-all-start = ((bf16[256,8,640]{2,1,0:T(8,128)(2,1)}), bf16[256,8,640]{2,1,0:T(8,128)(2,1)}, u32[]{:S(2)}, u32[]{:S(2)}) async-start(bf16[256,8,640]{2,1,0:T(8,128)(2,1)} %fusion.22), calls=%async_computation | async-start | bytes 5242880 | tf_op jit(solution)/shard_map/all_to_all | solution.py:45
  38.4 2.9 %copy.14 = f32[1024,512]{0,1:T(8,128)} copy(f32[1024,512]{1,0:T(8,128)} %param.13) | data formatting | bytes 4194304 | tf_op args[5]
  41.3 62.4 %all-to-all-done = bf16[256,8,640]{2,1,0:T(8,128)(2,1)} async-done(((bf16[256,8,640]{2,1,0:T(8,128)(2,1)}), bf16[256,8,640]{2,1,0:T(8,128)(2,1)}, u32[]{:S(2)}, u32[]{:S(2)}) %all-to-all-start) | async-done | bytes 2621472 | tf_op jit(solution)/shard_map/all_to_all | solution.py:45
  103.7 1.4 multiply_reduce_fusion
  105.1 0.0 copy-start.2
  105.1 0.0 copy-start.1
  105.1 5.1 %fusion.1 = f32[1024,640]{0,1:T(8,128)S(1)} fusion(s32[2048]{0:T(1024)S(1)} %convert_add_fusion, bf16[256,8,640]{2,1,0:T(8,128)(2,1)} %all-to-all-done), kind=kOutput, calls=%fused_computation.4 | convolution fusion | flops 2686451712 | bytes 5251072 | tf_op jit(solution)/shard_map/dot_general | solution.py:52
  110.2 0.0 copy-done.2
  110.3 0.0 copy-done.1
  110.3 0.0 copy-start.3
  110.3 3.7 %fusion.25 = bf16[256,8,512]{2,1,0:T(8,128)(2,1)} fusion(s32[2048]{0:T(1024)S(1)} %convert_add_fusion, f32[1024,640]{0,1:T(8,128)S(1)} %fusion.1, f32[1024,512]{0,1:T(8,128)S(1)} %copy-done.1, f32[1024]{0:T(1024)S(1)} %multiply_add_fusion), kind=kOutput, calls=%fused_computation.31 | convolution fusion | flops 2153250816 | bytes 6303744 | tf_op jit(solution)/shard_map/dot_general | solution.py:59
  114.0 6.8 %all-to-all-start.1 = ((bf16[256,8,512]{2,1,0:T(8,128)(2,1)}), bf16[256,8,512]{2,1,0:T(8,128)(2,1)}, u32[]{:S(2)}, u32[]{:S(2)}) async-start(bf16[256,8,512]{2,1,0:T(8,128)(2,1)} %fusion.25), calls=%async_computation.1 | async-start | bytes 4194304 | tf_op jit(solution)/shard_map/all_to_all | solution.py:71
  120.8 0.0 copy-done.3
  120.9 6.3 %add_divide_fusion = f32[1024,512]{0,1:T(8,128)} fusion(f32[1024,512]{0,1:T(8,128)} %copy.14, bf16[2048,640]{1,0:T(8,128)(2,1)} %bitcast.1, s32[2048]{0:T(1024)S(1)} %convert_add_fusion, f32[1024]{0:T(1024)S(1)} %multiply_add_fusion), kind=kOutput, calls=%fused_computation.27 | convolution fusion | flops 2151677952 | bytes 6303744 | tf_op jit(solution)/shard_map/dot_general | solution.py:64
  127.2 2.9 %copy.16 = f32[1024,512]{1,0:T(8,128)} copy(f32[1024,512]{0,1:T(8,128)} %add_divide_fusion) | data formatting | bytes 4194304
  130.1 43.4 %all-to-all-done.1 = bf16[256,8,512]{2,1,0:T(8,128)(2,1)} async-done(((bf16[256,8,512]{2,1,0:T(8,128)(2,1)}), bf16[256,8,512]{2,1,0:T(8,128)(2,1)}, u32[]{:S(2)}, u32[]{:S(2)}) %all-to-all-start.1) | async-done | bytes 2097184 | tf_op jit(solution)/shard_map/all_to_all | solution.py:71
  173.4 4.9 %fusion.26 = bf16[1024,512]{1,0:T(8,128)(2,1)} fusion(bf16[256,8,512]{2,1,0:T(8,128)(2,1)} %all-to-all-done.1, s32[1024]{0:T(1024)S(1)} %get-tuple-element.16), kind=kOutput, calls=%fused_computation.32 | convolution fusion | flops 2150105088 | bytes 3149824 | tf_op jit(solution)/shard_map/dot_general | solution.py:73
  (6 shorter events, 0.0 us)
Async XLA Ops:
  0.6 2.5 %copy-start = (bf16[3072,512]{1,0:T(8,128)(2,1)S(1)}, bf16[3072,512]{1,0:T(8,128)(2,1)}, u32[]{:S(2)}) copy-start(bf16[3072,512]{1,0:T(8,128)(2,1)} %param.11) | copy-start | bytes 9437188
  21.9 81.8 %all-to-all-start = ((bf16[256,8,640]{2,1,0:T(8,128)(2,1)}), bf16[256,8,640]{2,1,0:T(8,128)(2,1)}, u32[]{:S(2)}, u32[]{:S(2)}) async-start(bf16[256,8,640]{2,1,0:T(8,128)(2,1)} %fusion.22), calls=%async_computation | async-start | bytes 5242880 | tf_op jit(solution)/shard_map/all_to_all | solution.py:45
  105.1 5.2 %copy-start.2 = (f32[1024]{0:T(1024)S(1)}, f32[1024]{0:T(1024)}, u32[]{:S(2)}) copy-start(f32[1024]{0:T(1024)} %param.14) | copy-start | bytes 12292
  105.1 5.2 %copy-start.1 = (f32[1024,512]{0,1:T(8,128)S(1)}, f32[1024,512]{0,1:T(8,128)}, u32[]{:S(2)}) copy-start(f32[1024,512]{0,1:T(8,128)} %copy.14) | copy-start | bytes 6291460
  110.3 10.6 %copy-start.3 = (f32[1024]{0:T(1024)}, f32[1024]{0:T(1024)S(1)}, u32[]{:S(2)}) copy-start(f32[1024]{0:T(1024)S(1)} %multiply_add_fusion) | copy-start | bytes 12292
  114.0 59.5 %all-to-all-start.1 = ((bf16[256,8,512]{2,1,0:T(8,128)(2,1)}), bf16[256,8,512]{2,1,0:T(8,128)(2,1)}, u32[]{:S(2)}, u32[]{:S(2)}) async-start(bf16[256,8,512]{2,1,0:T(8,128)(2,1)} %fusion.25), calls=%async_computation.1 | async-start | bytes 4194304 | tf_op jit(solution)/shard_map/all_to_all | solution.py:71
